TPU v7x, 256 devices: a whole 4x4x8 slice. The times are simulated.
256 devices in a mesh: ta: 8 (over x_lo, y), gx: 4 (over x_hi, core), yz: 8 (over z).
Axes of the slice: x: 4 (x_hi: 2, x_lo: 2; x = x_hi * 2 + x_lo), y: 4, z: 8, core: 2. Of those that a mesh axis runs over, the one named last changes fastest.
Arguments:
- vectors: bfloat16 [2, 3, 32, 64, 256, 128], P(None, None, 'gx', 'yz', 'ta'), parts along dimension 4, may hold values from -6 to 6
- gauge_x: float32 [2, 3, 3, 32, 64, 256], P(None, None, None, 'gx', 'yz', 'ta'), parts along dimension 5, may hold values from -6 to 6
- gauge_y: float32 [2, 3, 3, 32, 64, 256], P(None, None, None, 'gx', 'yz', 'ta'), parts along dimension 5, may hold values from -6 to 6
Outputs:
- elementals: float32 [16, 2, 128, 128], P('ta'), parts along dimension 0
There are 8 independent parts, one for each index of `ta`. A program takes and returns all parts, laid end to end along the dimension named above; each array names one. Nothing has to cross between parts.
All inputs are finite; a program needn't handle non-finite values.
Results may differ from a plain program's by a relative error of at most 0.0029.
Values may be sent and summed in bfloat16 or wider, within the bound.
No kernel may reach another device: no remote copies, remote signals or barrier semaphores. Data moves between devices by JAX's collectives and lax.ppermute only.
A program may use at most 64 MiB of HBM per device.

v0:
```python
import math
import jax
import jax.numpy as jnp
from jax import lax
from jax.sharding import PartitionSpec as P


def shifted(value, axis, steps):
    count = lax.axis_size(axis)
    pairs = [(source, (source + steps) % count) for source in range(count)]
    return lax.ppermute(value, axis, pairs)


def colour_apply(gauge, source_vectors):
    real_parts = []
    imag_parts = []
    for colour in range(3):
        real_running = jnp.zeros(source_vectors.shape[2:], jnp.float32)
        imaginary_running = jnp.zeros(source_vectors.shape[2:], jnp.float32)
        for inner_product in range(3):
            left_real = gauge[0, colour, inner_product][..., None]
            left_imaginary = gauge[1, colour, inner_product][..., None]
            right_real = source_vectors[0, inner_product].astype(jnp.float32)
            right_imaginary = source_vectors[1, inner_product].astype(jnp.float32)
            real_running = real_running + left_real * right_real - left_imaginary * right_imaginary
            imaginary_running = (
                imaginary_running + left_real * right_imaginary + left_imaginary * right_real
            )
        real_parts.append(real_running)
        imag_parts.append(imaginary_running)
    return jnp.stack([jnp.stack(real_parts), jnp.stack(imag_parts)]).astype(jnp.bfloat16)


def right_block(image):
    nvecs = image.shape[-1]
    real_rows = image[0].reshape(-1, nvecs)
    imag_rows = image[1].reshape(-1, nvecs)
    first = jnp.concatenate([real_rows, imag_rows], 0)
    second = jnp.concatenate([imag_rows, -real_rows], 0)
    return (first, second)


def contract(left_cols, right_cols):
    return lax.dot_general(
        left_cols, right_cols, (((0,), (0,)), ((), ())), preferred_element_type=jnp.float32
    )


def local(vectors, gauge_x, gauge_y):
    nvecs = vectors.shape[-1]
    from_next_x = shifted(vectors[:, :, :1], "gx", -1)
    shifted_x = jnp.concatenate([vectors[:, :, 1:], from_next_x], 2)
    from_next_y = shifted(vectors[:, :, :, :1], "yz", -1)
    shifted_y = jnp.concatenate([vectors[:, :, :, 1:], from_next_y], 3)
    image_x = colour_apply(gauge_x, shifted_x)
    image_y = colour_apply(gauge_y, shifted_y)
    left_rows = vectors.reshape(-1, nvecs)
    blocks = right_block(image_x) + right_block(image_y)
    summed = lax.psum(
        jnp.concatenate([contract(left_rows, member) for member in blocks], 1), ("gx", "yz")
    )
    sites_total = (
        vectors.shape[2]
        * lax.axis_size("gx")
        * vectors.shape[3]
        * lax.axis_size("yz")
        * vectors.shape[4]
    )
    scaling = 1.0 / math.sqrt(3.0 * sites_total)
    return (summed * scaling).reshape(nvecs, 2, 2, nvecs).transpose(1, 2, 0, 3)


def solution(mesh):
    placed = (
        P(None, None, "gx", "yz", "ta", None),
        P(None, None, None, "gx", "yz", "ta"),
        P(None, None, None, "gx", "yz", "ta"),
    )
    return jax.shard_map(
        local, mesh=mesh, in_specs=placed, out_specs=P("ta", None, None, None), check_vma=False
    )
```

profile of v0, /device:TPU:8, one launch (start us, length us, event | category | flops | bytes accessed | tf_op | source)
XLA Modules:
  0.0 315.3 jit_solution(16234775033811610859)
XLA Ops:
  6.5 0.0 all-reduce.2.cloned.1.call-start
  6.5 1.0 slice.186
  7.6 0.0 copy-start
  7.6 2.5 collective-permute-start
  10.1 1.0 slice.212
  11.1 5.9 %collective-permute-start.1 = (bf16[2,3,8,1,32,128]{5,4,3,2,1,0:T(8,128)(2,1)S(1)}, bf16[2,3,8,1,32,128]{5,4,3,2,1,0:T(8,128)(2,1)S(1)}, u32[]{:S(2)}, u32[]{:S(2)}) collective-permute-start(bf16[2,3,8,1,32,128]{5,4,3,2,1,0:T(8,128)(2,1)S(1)} %slice.212), channel_id=1, source_target_pairs={{0,7},{1,0},{2,1},{3,2},{4,3},{5,4},{6,5},{7,6},{8,15},{9,8},{10,9... | collective-permute-start | bytes 1179656 | tf_op jit(solution)/shard_map/ppermute | solution.py:11
  17.1 0.0 copy-done
  17.1 0.0 copy-start.1
  17.1 0.0 copy-start.2
  17.1 0.0 slice-start
  17.1 0.7 slice.211
  17.8 0.4 copy-done.1
  18.2 0.1 copy-done.2
  18.4 0.0 collective-permute-done
  18.4 0.8 slice-done
  19.2 2.1 fusion.51
  21.3 1.9 fusion.33
  23.3 3.9 %fusion.57 = (bf16[1,8,8,32,128]{4,3,2,1,0:T(8,128)(2,1)S(1)}, bf16[1,8,8,32,128]{4,3,2,1,0:T(8,128)(2,1)S(1)}, bf16[1,8,8,32,128]{4,3,2,1,0:T(8,128)(2,1)S(1)}, bf16[1,8,8,32,128]{4,3,2,1,0:T(8,128)(2,1)S(1)}) fusion(bf16[1,8,8,32,128]{4,3,2,1,0:T(8,128)(2,1)S(1)} %get-tuple-element.11, bf16[1,8,8,32,128]{4,3,2,1,0:T(8,128)(2,1)S(1)} %get-tuple-element.10, ...), kind=kLoop, calls=%fused_computation.145 | loop fusion | flops 14155776 | bytes 5341184 | tf_op jit(solution)/shard_map/convert.26
  27.2 0.3 pad_maximum_fusion
  27.5 0.3 bitcast_negate_fusion.1
  27.8 1.0 fusion.25
  28.9 1.0 fusion.22
  29.9 0.0 collective-permute-done.1
  29.9 2.0 fusion.87
  31.9 1.9 fusion.69
  33.9 3.9 %fusion.93 = (bf16[1,8,8,32,128]{4,3,2,1,0:T(8,128)(2,1)S(1)}, bf16[1,8,8,32,128]{4,3,2,1,0:T(8,128)(2,1)S(1)}, bf16[1,8,8,32,128]{4,3,2,1,0:T(8,128)(2,1)S(1)}, bf16[1,8,8,32,128]{4,3,2,1,0:T(8,128)(2,1)S(1)}) fusion(bf16[1,8,8,32,128]{4,3,2,1,0:T(8,128)(2,1)S(1)} %get-tuple-element.18, bf16[1,8,8,32,128]{4,3,2,1,0:T(8,128)(2,1)S(1)} %get-tuple-element.17, ...), kind=kLoop, calls=%fused_computation.181 | loop fusion | flops 14155776 | bytes 5341184 | tf_op jit(solution)/shard_map/convert.16
  37.8 0.3 pad_maximum_fusion.2
  38.2 0.3 bitcast_negate_fusion
  38.5 1.0 fusion.19
  39.5 1.1 fusion.16
  40.6 0.7 pad_maximum_fusion.6
  41.3 0.0 all-reduce.2.cloned.1.call-update
  41.3 265.3 %all-reduce.2.cloned.1.call-done = f32[128,512]{0,1:T(8,128)} async-done(((f32[128,512]{0,1:T(8,128)}), f32[128,512]{0,1:T(8,128)}) %all-reduce.2.cloned.1.call-update) | async-done | bytes 262160 | tf_op jit(solution)/shard_map/psum | solution.py:59
  306.6 1.0 broadcast_multiply_fusion
  307.6 0.8 copy.4
  (2 shorter events, 0.1 us)
Async XLA Ops:
  6.5 300.1 %all-reduce.2.cloned.1.call-start = ((), (), s32[]{:S(2)}) async-start(), calls=%async_computation | async-start | bytes 524288 | tf_op jit(solution)/shard_map/psum | solution.py:59
  7.6 9.5 %copy-start = (bf16[2,3,8,8,32,128]{5,4,3,2,1,0:T(8,128)(2,1)S(1)}, bf16[2,3,8,8,32,128]{5,4,3,2,1,0:T(8,128)(2,1)}, u32[]{:S(2)}) copy-start(bf16[2,3,8,8,32,128]{5,4,3,2,1,0:T(8,128)(2,1)} %param.3) | copy-start | bytes 9437188
  7.6 10.8 %collective-permute-start = (bf16[2,3,1,8,32,128]{5,4,3,2,1,0:T(8,128)(2,1)S(1)}, bf16[2,3,1,8,32,128]{5,4,3,2,1,0:T(8,128)(2,1)S(1)}, u32[]{:S(2)}, u32[]{:S(2)}) collective-permute-start(bf16[2,3,1,8,32,128]{5,4,3,2,1,0:T(8,128)(2,1)S(1)} %slice.186), channel_id=1, source_target_pairs={{0,24},{8,0},{16,8},{24,16},{1,25},{9,1},{17,9},{25,17},{2,26},{10... | collective-permute-start | bytes 1179656 | tf_op jit(solution)/shard_map/ppermute | solution.py:11
  11.1 18.8 %collective-permute-start.1 = (bf16[2,3,8,1,32,128]{5,4,3,2,1,0:T(8,128)(2,1)S(1)}, bf16[2,3,8,1,32,128]{5,4,3,2,1,0:T(8,128)(2,1)S(1)}, u32[]{:S(2)}, u32[]{:S(2)}) collective-permute-start(bf16[2,3,8,1,32,128]{5,4,3,2,1,0:T(8,128)(2,1)S(1)} %slice.212), channel_id=1, source_target_pairs={{0,7},{1,0},{2,1},{3,2},{4,3},{5,4},{6,5},{7,6},{8,15},{9,8},{10,9... | collective-permute-start | bytes 1179656 | tf_op jit(solution)/shard_map/ppermute | solution.py:11
  17.1 1.1 copy-start.1
  17.1 1.2 copy-start.2
  17.1 2.1 slice-start
Sparse Core Ops, SparseCore 0:
  41.5 265.1 all-reduce.1
where the time goes:
time: 315 us
  waiting for transfers between devices  265 us (84%)
  other arithmetic  18.8 us (6%)
  between operations  13.6 us (4%)
  starting transfers between devices  8.47 us (3%)
  local copies, waits for them, and re-layouts  5 us (2%)
  matrix products  4.18 us (1%)
    psum x1, waiting for transfers between devices, local(): lax.psum(jnp.concatenate([contract(left_rows, member) for member in block...  265 us
    another operation x6, other arithmetic  15.8 us
    ppermute x2, starting transfers between devices, shifted(): return lax.ppermute(value, axis, pairs)  8.47 us
  transfers between devices with their start and end apart: 3, of which 1 were waited for; matrix products, arithmetic and copies ran while one was open for 4% of the time, Pallas kernels for 0%

commit v1 on v0

--- a/solution.py
+++ b/solution.py
@@ -56,9 +56,9 @@
     image_y = colour_apply(gauge_y, shifted_y)
     left_rows = vectors.reshape(-1, nvecs)
     blocks = right_block(image_x) + right_block(image_y)
-    summed = lax.psum(
-        jnp.concatenate([contract(left_rows, member) for member in blocks], 1), ("gx", "yz")
-    )
+    summed = jnp.concatenate([contract(left_rows, member) for member in blocks], 1)
+    for mesh_axis in ("yz", "gx"):
+        summed = lax.psum(summed, mesh_axis)
     sites_total = (
         vectors.shape[2]
         * lax.axis_size("gx")

time: 315 us -> 171 us (0.54)
  waiting for transfers between devices: 265 us -> 119 us
    psum x1 -> x2, waiting for transfers between devices: 265 us -> 119 us  [local(): summed = lax.psum(summed, mesh_axis)]
  transfers between devices with their start and end apart: 3 -> 4, of which waited for: 1 -> 2; matrix products, arithmetic and copies ran while one was open for 4% -> 7% of each run, Pallas kernels for 0% -> 0%
where the time goes in v1:
time: 171 us; the launch traced here: 169 us
  waiting for transfers between devices  119 us (70%)
  other arithmetic  18.8 us (11%)
  between operations  13.6 us (8%)
  starting transfers between devices  8.52 us (5%)
  local copies, waits for them, and re-layouts  5 us (3%)
  matrix products  4.18 us (2%)
    psum x2, waiting for transfers between devices, local(): summed = lax.psum(summed, mesh_axis)  119 us
    another operation x6, other arithmetic  15.8 us
    ppermute x2, starting transfers between devices, shifted(): return lax.ppermute(value, axis, pairs)  8.47 us
    dot_general x4, matrix products, contract(): lax.dot_general(left_cols, right_cols, (((0,), (0,)), ((), ())), preferre...  4.18 us
  transfers between devices with their start and end apart: 4, of which 2 were waited for; matrix products, arithmetic and copies ran while one was open for 7% of the time, Pallas kernels for 0%

profile of v1, /device:TPU:8, one launch (start us, length us, event | category | flops | bytes accessed | tf_op | source)
XLA Modules:
  0.0 169.0 jit_solution(5933804391679605913)
XLA Ops:
  6.5 0.0 all-reduce.3.cloned.1.call-start
  6.5 1.0 slice.186
  7.6 0.0 copy-start
  7.6 2.5 %collective-permute-start = (bf16[2,3,1,8,32,128]{5,4,3,2,1,0:T(8,128)(2,1)S(1)}, bf16[2,3,1,8,32,128]{5,4,3,2,1,0:T(8,128)(2,1)S(1)}, u32[]{:S(2)}, u32[]{:S(2)}) collective-permute-start(bf16[2,3,1,8,32,128]{5,4,3,2,1,0:T(8,128)(2,1)S(1)} %slice.186), channel_id=1, source_target_pairs={{0,24},{8,0},{16,8},{24,16},{1,25},{9,1},{17,9},{25,17},{2,26},{10... | collective-permute-start | bytes 1179656 | tf_op jit(solution)/shard_map/ppermute | solution.py:11
  10.1 1.0 slice.212
  11.1 5.9 %collective-permute-start.1 = (bf16[2,3,8,1,32,128]{5,4,3,2,1,0:T(8,128)(2,1)S(1)}, bf16[2,3,8,1,32,128]{5,4,3,2,1,0:T(8,128)(2,1)S(1)}, u32[]{:S(2)}, u32[]{:S(2)}) collective-permute-start(bf16[2,3,8,1,32,128]{5,4,3,2,1,0:T(8,128)(2,1)S(1)} %slice.212), channel_id=1, source_target_pairs={{0,7},{1,0},{2,1},{3,2},{4,3},{5,4},{6,5},{7,6},{8,15},{9,8},{10,9... | collective-permute-start | bytes 1179656 | tf_op jit(solution)/shard_map/ppermute | solution.py:11
  17.1 0.0 copy-done
  17.1 0.0 copy-start.1
  17.1 0.0 copy-start.2
  17.1 0.0 slice-start
  17.1 0.7 slice.211
  17.8 0.4 copy-done.1
  18.2 0.1 copy-done.2
  18.4 0.0 collective-permute-done
  18.4 0.8 slice-done
  19.2 2.1 %fusion.51 = (bf16[1,8,8,32,128]{4,3,2,1,0:T(8,128)(2,1)S(1)}, bf16[1,8,8,32,128]{4,3,2,1,0:T(8,128)(2,1)S(1)}, bf16[1,8,8,32,128]{4,3,2,1,0:T(8,128)(2,1)S(1)},...) fusion(f32[8,8,32]{2,1,0:T(8,128)S(1)} %get-tuple-element.41, ...), kind=kLoop, calls=%fused_computation.139 | loop fusion | flops 6291456 | bytes 6864896 | tf_op jit(solution)/shard_map/convert.25
  21.3 1.9 %fusion.33 = bf16[1,8,8,32,128]{4,3,2,1,0:T(8,128)(2,1)S(1)} fusion(bf16[1,8,8,32,128]{4,3,2,1,0:T(8,128)(2,1)S(1)} %get-tuple-element.11, bf16[1,8,8,32,128]{4,3,2,1,0:T(8,128)(2,1)S(1)} %get-tuple-element.10, bf16[1,8,8,32,128]{4,3,2,1,0:T(8,128)(2,1)S(1)} %get-tuple-element.9, bf16[1,8,8,32,128]{4,3,2,1,0:T(8,128)(2,1)S(1)} %get-tuple-element.8, ...), kind=kLoop, calls=%fused_computation.121 | loop fusion | flops 4718592 | bytes 3719168 | tf_op jit(solution)/shard_map/convert.29
  23.3 3.9 %fusion.57 = (bf16[1,8,8,32,128]{4,3,2,1,0:T(8,128)(2,1)S(1)}, bf16[1,8,8,32,128]{4,3,2,1,0:T(8,128)(2,1)S(1)}, bf16[1,8,8,32,128]{4,3,2,1,0:T(8,128)(2,1)S(1)}, bf16[1,8,8,32,128]{4,3,2,1,0:T(8,128)(2,1)S(1)}) fusion(bf16[1,8,8,32,128]{4,3,2,1,0:T(8,128)(2,1)S(1)} %get-tuple-element.11, bf16[1,8,8,32,128]{4,3,2,1,0:T(8,128)(2,1)S(1)} %get-tuple-element.10, ...), kind=kLoop, calls=%fused_computation.145 | loop fusion | flops 14155776 | bytes 5341184 | tf_op jit(solution)/shard_map/convert.26
  27.2 0.3 pad_maximum_fusion
  27.5 0.3 bitcast_negate_fusion.1
  27.8 1.0 fusion.25
  28.9 1.0 fusion.22
  29.9 0.0 collective-permute-done.1
  29.9 2.0 %fusion.87 = (bf16[1,8,8,32,128]{4,3,2,1,0:T(8,128)(2,1)S(1)}, bf16[1,8,8,32,128]{4,3,2,1,0:T(8,128)(2,1)S(1)}, bf16[1,8,8,32,128]{4,3,2,1,0:T(8,128)(2,1)S(1)},...) fusion(f32[8,8,32]{2,1,0:T(8,128)S(1)} %get-tuple-element.59, ...), kind=kLoop, calls=%fused_computation.175 | loop fusion | flops 6291456 | bytes 6864896 | tf_op jit(solution)/shard_map/convert.15
  31.9 1.9 %fusion.69 = bf16[1,8,8,32,128]{4,3,2,1,0:T(8,128)(2,1)S(1)} fusion(bf16[1,8,8,32,128]{4,3,2,1,0:T(8,128)(2,1)S(1)} %get-tuple-element.18, bf16[1,8,8,32,128]{4,3,2,1,0:T(8,128)(2,1)S(1)} %get-tuple-element.17, bf16[1,8,8,32,128]{4,3,2,1,0:T(8,128)(2,1)S(1)} %get-tuple-element.16, bf16[1,8,8,32,128]{4,3,2,1,0:T(8,128)(2,1)S(1)} %get-tuple-element.15, ...), kind=kLoop, calls=%fused_computation.157 | loop fusion | flops 4718592 | bytes 3719168 | tf_op jit(solution)/shard_map/convert.19
  33.9 3.9 %fusion.93 = (bf16[1,8,8,32,128]{4,3,2,1,0:T(8,128)(2,1)S(1)}, bf16[1,8,8,32,128]{4,3,2,1,0:T(8,128)(2,1)S(1)}, bf16[1,8,8,32,128]{4,3,2,1,0:T(8,128)(2,1)S(1)}, bf16[1,8,8,32,128]{4,3,2,1,0:T(8,128)(2,1)S(1)}) fusion(bf16[1,8,8,32,128]{4,3,2,1,0:T(8,128)(2,1)S(1)} %get-tuple-element.18, bf16[1,8,8,32,128]{4,3,2,1,0:T(8,128)(2,1)S(1)} %get-tuple-element.17, ...), kind=kLoop, calls=%fused_computation.181 | loop fusion | flops 14155776 | bytes 5341184 | tf_op jit(solution)/shard_map/convert.16
  37.8 0.3 pad_maximum_fusion.2
  38.2 0.3 bitcast_negate_fusion
  38.5 1.0 fusion.19
  39.5 1.1 fusion.16
  40.6 0.7 pad_maximum_fusion.6
  41.3 0.0 all-reduce.3.cloned.1.call-update
  41.3 0.0 all-reduce.5.cloned.1.call-start
  41.4 72.1 %all-reduce.3.cloned.1.call-done = f32[128,512]{0,1:T(8,128)} async-done(((f32[128,512]{0,1:T(8,128)}), f32[128,512]{0,1:T(8,128)}) %all-reduce.3.cloned.1.call-update) | async-done | bytes 262160 | tf_op jit(solution)/shard_map/psum | solution.py:61
  113.5 0.0 all-reduce.5.cloned.1.call-update
  113.5 46.9 %all-reduce.5.cloned.1.call-done = f32[128,512]{0,1:T(8,128)} async-done(((f32[128,512]{0,1:T(8,128)}), f32[128,512]{0,1:T(8,128)}) %all-reduce.5.cloned.1.call-update) | async-done | bytes 262160 | tf_op jit(solution)/shard_map/psum | solution.py:61
  160.4 1.0 broadcast_multiply_fusion
  161.4 0.8 copy.4
  (2 shorter events, 0.1 us)
Async XLA Ops:
  6.5 106.9 %all-reduce.3.cloned.1.call-start = ((), (), s32[]{:S(2)}) async-start(), calls=%async_computation | async-start | bytes 524288 | tf_op jit(solution)/shard_map/psum | solution.py:61
  7.6 9.5 %copy-start = (bf16[2,3,8,8,32,128]{5,4,3,2,1,0:T(8,128)(2,1)S(1)}, bf16[2,3,8,8,32,128]{5,4,3,2,1,0:T(8,128)(2,1)}, u32[]{:S(2)}) copy-start(bf16[2,3,8,8,32,128]{5,4,3,2,1,0:T(8,128)(2,1)} %param.3) | copy-start | bytes 9437188
  7.6 10.8 %collective-permute-start = (bf16[2,3,1,8,32,128]{5,4,3,2,1,0:T(8,128)(2,1)S(1)}, bf16[2,3,1,8,32,128]{5,4,3,2,1,0:T(8,128)(2,1)S(1)}, u32[]{:S(2)}, u32[]{:S(2)}) collective-permute-start(bf16[2,3,1,8,32,128]{5,4,3,2,1,0:T(8,128)(2,1)S(1)} %slice.186), channel_id=1, source_target_pairs={{0,24},{8,0},{16,8},{24,16},{1,25},{9,1},{17,9},{25,17},{2,26},{10... | collective-permute-start | bytes 1179656 | tf_op jit(solution)/shard_map/ppermute | solution.py:11
  11.1 18.8 %collective-permute-start.1 = (bf16[2,3,8,1,32,128]{5,4,3,2,1,0:T(8,128)(2,1)S(1)}, bf16[2,3,8,1,32,128]{5,4,3,2,1,0:T(8,128)(2,1)S(1)}, u32[]{:S(2)}, u32[]{:S(2)}) collective-permute-start(bf16[2,3,8,1,32,128]{5,4,3,2,1,0:T(8,128)(2,1)S(1)} %slice.212), channel_id=1, source_target_pairs={{0,7},{1,0},{2,1},{3,2},{4,3},{5,4},{6,5},{7,6},{8,15},{9,8},{10,9... | collective-permute-start | bytes 1179656 | tf_op jit(solution)/shard_map/ppermute | solution.py:11
  17.1 1.1 copy-start.1
  17.1 1.2 copy-start.2
  17.1 2.1 %slice-start = ((bf16[2,3,8,8,32,128]{5,4,3,2,1,0:T(8,128)(2,1)}), bf16[2,3,7,8,32,128]{5,4,3,2,1,0:T(8,128)(2,1)S(1)}, s32[]{:S(2)}) async-start(bf16[2,3,8,8,32,128]{5,4,3,2,1,0:T(8,128)(2,1)} %param.3), calls=%async_computation.2 | async-start | bytes 5505024 | tf_op jit(solution)/shard_map/slice | solution.py:52
  41.3 119.0 %all-reduce.5.cloned.1.call-start = ((), (), s32[]{:S(2)}) async-start(), calls=%async_computation.1 | async-start | bytes 524288 | tf_op jit(solution)/shard_map/psum | solution.py:61
Sparse Core Ops, SparseCore 0:
  41.5 71.9 all-reduce.2
  116.3 44.0 all-reduce.4
